TPU v7x, 256 devices: a whole 4x4x8 slice. The times are simulated.
256 devices in a mesh: ctx: 32 (over y, x, core), exp: 8 (over z).
Axes of the slice: x: 4, y: 4, z: 8, core: 2. Of those that a mesh axis runs over, the one named last changes fastest.
Arguments:
- ssm_input: bfloat16 [4096, 4096], P('ctx', 'exp'), may hold values from -6 to 6
- gate_input: bfloat16 [4096, 4096], P('ctx', 'exp'), may hold values from -6 to 6
- key_proj: bfloat16 [4096, 128], P('ctx'), may hold values from -4 to 4
- query_proj: bfloat16 [4096, 128], P('ctx'), may hold values from -4 to 4
- step_size: float32 [4096, 64], P('ctx', 'exp'), may hold values from 0 to 1, as said below
- decay_rate: float32 [64], P('exp'), may hold values from 0.5 to 1.5
- head_gain: float32 [4096], P('exp'), may hold values from 0.5 to 1.5
- residual: bfloat16 [4096, 4096], P('ctx', 'exp'), may hold values from -33 to 33
- ffn_gain: float32 [4096], replicated, may hold values from 0.5 to 1.5
- gate_weight: bfloat16 [8, 4096, 12288], P('exp', None, 'ctx'), may hold values from -0.09375 to 0.09375
- up_weight: bfloat16 [8, 4096, 12288], P('exp', None, 'ctx'), may hold values from -0.09375 to 0.09375
- down_weight: bfloat16 [8, 12288, 4096], P('exp', 'ctx'), may hold values from -0.0546875 to 0.0546875
- expert_ids: int32 [4096, 2], P('ctx'), may hold values from 0 to 7, all different within a row; in each aligned block of 128 rows (0 to 127, 128 to 255, ...) at most 48 rows name the same one
- route_weight: float32 [4096, 2], P('ctx'), may hold values from 0.5 to 2
Outputs:
- block_out: bfloat16 [4096, 4096], P('ctx', 'exp')
- expert_out: bfloat16 [4096, 4096], P('ctx', 'exp')
Inputs may be any that keep to these rules, and one draw needn't show every extreme that they name: `step_size`: step sizes are positive. `expert_ids`: the two experts of a token differ. In each aligned block of 128 rows (the tokens of one shard) no expert is named by more than 48 rows, and in some block one expert is named by exactly 48 rows.
All inputs are finite; a program needn't handle non-finite values.
Results may differ from a plain program's by a relative error of at most 0.022.
Values may be sent and summed in bfloat16 or wider, within the bound.
No kernel may reach another device: no remote copies, remote signals or barrier semaphores. Data moves between devices by JAX's collectives and lax.ppermute only.
A program may use at most 128 MiB of HBM per device.

v0:
```python
import jax
import jax.numpy as jnp
from jax import lax
from jax.sharding import PartitionSpec as P

precise = lax.Precision.HIGHEST


def carried_in(shard, axis, combine, identity):
    length, mine = (lax.axis_size(axis), lax.axis_index(axis))
    everything = jax.tree.map(
        lambda part, kind: lax.all_gather(part.astype(kind), axis),
        shard,
        (jnp.bfloat16, jnp.bfloat16),
    )
    start = jax.tree.map(
        lambda part, zero: jnp.broadcast_to(jnp.asarray(zero, part.dtype), part.shape),
        shard,
        identity,
    )

    def lap(k, before):
        reached = k < mine
        new = combine(
            before, jax.tree.map(lambda part, own: part[k].astype(own.dtype), everything, shard)
        )
        return jax.tree.map(lambda a, b: jnp.where(reached, a, b), new, before)

    return lax.fori_loop(0, length, lap, start)


def local_block(ssm_piece, key_piece, query_piece, step_piece, decay_rate, head_count):
    row_count = ssm_piece.shape[0]
    head_width = ssm_piece.shape[1] // head_count
    values = ssm_piece.astype(jnp.float32).reshape(row_count, head_count, head_width)
    key_vals = key_piece.astype(jnp.float32)
    queries = query_piece.astype(jnp.float32)
    log_steps = -step_piece * decay_rate[None, :]
    running = jnp.cumsum(log_steps, axis=0)
    scores = jnp.dot(queries, key_vals.T, precision=precise)
    causal = (jnp.arange(row_count)[:, None] >= jnp.arange(row_count)[None, :])[:, :, None]
    spacing = running[:, None, :] - running[None, :, :]
    decays = jnp.where(causal, jnp.exp(jnp.where(causal, spacing, 0.0)), 0.0)
    within = jnp.einsum("tsh,ts,shp->thp", decays, scores, values, precision=precise)
    overall = running[-1]
    fading = jnp.exp(overall[None, :] - running)
    states = jnp.einsum("sh,shp,sn->hpn", fading, values, key_vals, precision=precise)
    return (within, running, overall, states)


def route_tables(expert_ids, route_weight, experts, capacity):
    matched = expert_ids[None, :, :] == experts[:, None, None]
    member = jnp.any(matched, axis=2).astype(jnp.int32)
    gate_sum = jnp.sum(jnp.where(matched, route_weight[None, :, :], 0.0), axis=2)
    slot_index = jnp.cumsum(member, axis=1) - 1
    positions = jnp.arange(capacity, dtype=jnp.int32)
    routing = (
        (slot_index[:, None, :] == positions[None, :, None]) & (member[:, None, :] > 0)
    ).astype(jnp.float32)
    slot_weight = jnp.einsum("nkt,nt->nk", routing, gate_sum, precision=precise)
    return (routing, slot_weight)


def join_states(earlier, later):
    return (earlier[0] + later[0], jnp.exp(later[0])[:, None, None] * earlier[1] + later[1])


def on_device(
    ssm_input,
    gate_input,
    key_proj,
    query_proj,
    step_size,
    decay_rate,
    head_gain,
    residual,
    ffn_gain,
    gate_weight,
    up_weight,
    down_weight,
    expert_ids,
    route_weight,
):
    head_count = step_size.shape[1]
    row_count, channels = ssm_input.shape
    head_width = channels // head_count
    within, running, overall, states = local_block(
        ssm_input, key_proj, query_proj, step_size, decay_rate, head_count
    )
    prefix = carried_in(
        (overall, states), "ctx", join_states, (jnp.zeros_like(overall), jnp.zeros_like(states))
    )
    before = prefix[1]
    carried = jnp.einsum(
        "th,hpn,tn->thp",
        jnp.exp(running),
        before,
        query_proj.astype(jnp.float32),
        precision=precise,
    )
    mixer_out = within + carried
    gated_out = mixer_out * jax.nn.silu(gate_input.astype(jnp.float32)).reshape(
        row_count, head_count, head_width
    )
    inv_rms = lax.rsqrt(jnp.mean(gated_out * gated_out, axis=2, keepdims=True) + 1e-05)
    normed = (gated_out * inv_rms).reshape(row_count, channels) * head_gain[None, :]
    block_out = (residual.astype(jnp.float32) + normed).astype(jnp.bfloat16)
    owner_index = lax.axis_index("exp")
    exp_count = lax.axis_size("exp")
    capacity = 3 * row_count // exp_count
    tables, weights_all = route_tables(
        expert_ids, route_weight, jnp.arange(exp_count, dtype=jnp.int32), capacity
    )
    own_table = lax.dynamic_index_in_dim(tables, owner_index, 0, keepdims=False)
    own_weight = lax.dynamic_index_in_dim(weights_all, owner_index, 0, keepdims=False)
    gathered = lax.all_gather(block_out, "exp", axis=1, tiled=True)
    widened = gathered.astype(jnp.float32)
    ffn_input = (
        widened
        * lax.rsqrt(jnp.mean(widened * widened, axis=1, keepdims=True) + 1e-06)
        * ffn_gain[None, :]
    ).astype(jnp.bfloat16)
    chosen = jnp.dot(
        own_table.astype(jnp.bfloat16), ffn_input, preferred_element_type=jnp.float32
    ).astype(jnp.bfloat16)
    gate_here = gate_weight[0]
    up_here = up_weight[0]
    down_here = down_weight[0]
    token_piece = lax.all_gather(chosen, "ctx", axis=0, tiled=True)
    gate_proj = jnp.dot(token_piece, gate_here, preferred_element_type=jnp.float32)
    up_proj = jnp.dot(token_piece, up_here, preferred_element_type=jnp.float32)
    hidden = (jax.nn.silu(gate_proj) * up_proj).astype(jnp.bfloat16)
    summed = lax.psum_scatter(
        jnp.dot(hidden, down_here, preferred_element_type=jnp.float32).astype(jnp.bfloat16),
        "ctx",
        scatter_dimension=0,
        tiled=True,
    )
    spread = jnp.dot(
        own_table.T, own_weight[:, None] * summed.astype(jnp.float32), precision=precise
    )
    expert_out = lax.psum_scatter(
        spread.astype(jnp.bfloat16), "exp", scatter_dimension=1, tiled=True
    )
    return (block_out, expert_out)


def solution(mesh):
    placed = (
        P("ctx", "exp"),
        P("ctx", "exp"),
        P("ctx", None),
        P("ctx", None),
        P("ctx", "exp"),
        P("exp"),
        P("exp"),
        P("ctx", "exp"),
        P(),
        P("exp", None, "ctx"),
        P("exp", None, "ctx"),
        P("exp", "ctx", None),
        P("ctx", None),
        P("ctx", None),
    )
    return jax.shard_map(
        on_device,
        mesh=mesh,
        in_specs=placed,
        out_specs=(P("ctx", "exp"), P("ctx", "exp")),
        check_vma=False,
    )
```

profile of v0, /device:TPU:2, one launch (start us, length us, event | category | flops | bytes accessed | tf_op | source)
XLA Modules:
  0.0 405.1 jit_solution(16318344379442239635)
XLA Ops:
  9.1 1.0 copy.54
  10.2 1.7 convolution_convert_fusion.3
  12.7 21.7 %all-gather.1 = bf16[32,1,8]{2,1,0:T(2,128)(2,1)S(1)} all-gather(bf16[1,1,8]{2,1,0:T(2,128)(2,1)S(1)} %convert_bitcast_fusion), channel_id=1, replica_groups=mesh['ctx'=32,'exp'=8] {'ctx'}, dimensions={0}, use_global_device_ids=true | all-gather | bytes 528 | tf_op jit(solution)/shard_map/all_gather | solution.py:12
  35.2 1.7 convert_multiply_fusion.2
  36.9 1.8 copy.59
  39.3 1.6 fusion.52
  40.8 24.9 %all-gather.10.cloned.1.call-done = bf16[256,64,128]{2,1,0:T(8,128)(2,1)} async-done(((bf16[8,64,128]{2,1,0:T(8,128)(2,1)}), bf16[256,64,128]{2,1,0:T(8,128)(2,1)}) %all-gather.10.cloned.1.call-update) | async-done | bytes 4194320 | tf_op jit(solution)/shard_map/all_gather | solution.py:12
  65.8 33.8 %while.14 = (s32[]{:T(128)}, f32[8,64,128]{2,1,0:T(8,128)S(1)}, s32[]{:T(128)}, bf16[32,8]{1,0:T(8,128)(2,1)S(1)}, bf16[32,8,64,128]{3,2,1,0:T(8,128)(2,1)}, /*index=5*/s32[]{:T(128)}, s32[]{:T(128)}) while((s32[]{:T(128)}, f32[8,64,128]{2,1,0:T(8,128)S(1)}, s32[]{:T(128)}, bf16[32,8]{1,0:T(8,128)(2,1)S(1)}, ...), condition=%wide.region_2.3_spmd.clone, body=%wide.region_1.2_spmd.clone.sunk | while | flops 327692 | bytes 655545 | solution.py:29
  65.8 1.0 fusion.63
  66.8 1.0 fusion.63
  67.9 1.0 fusion.63
  68.9 1.0 fusion.63
  70.0 1.0 fusion.63
  71.0 1.0 fusion.63
  72.1 1.0 fusion.63
  73.2 1.0 fusion.63
  74.2 1.0 fusion.63
  75.3 1.0 fusion.63
  76.3 1.0 fusion.63
  77.4 1.0 fusion.63
  78.4 1.0 fusion.63
  79.5 1.0 fusion.63
  80.5 1.0 fusion.63
  81.6 1.0 fusion.63
  82.7 1.0 fusion.63
  83.7 1.0 fusion.63
  84.8 1.0 fusion.63
  85.8 1.0 fusion.63
  86.9 1.0 fusion.63
  89.0 1.0 fusion.63
  91.1 1.0 fusion.63
  92.2 1.0 fusion.63
  93.2 1.0 fusion.63
  94.3 1.0 fusion.63
  96.4 1.0 fusion.63
  98.5 1.0 fusion.63
  99.5 1.0 fusion.16
  100.6 1.8 multiply_reduce_fusion
  103.3 1.7 add_convert_fusion
  105.4 37.9 %all-gather.6.cloned.1.call-done = bf16[128,4096]{1,0:T(8,128)(2,1)} async-done(((bf16[128,512]{1,0:T(8,128)(2,1)}), bf16[128,4096]{1,0:T(8,128)(2,1)}) %all-gather.6.cloned.1.call-update) | async-done | bytes 1048592 | tf_op jit(solution)/shard_map/all_gather | solution.py:116
  143.4 1.5 fusion.10
  144.9 2.5 convolution_convert_fusion.2
  147.5 66.3 %all-gather.8.cloned.1.call-done = bf16[1536,4096]{1,0:T(8,128)(2,1)} async-done(((bf16[48,4096]{1,0:T(8,128)(2,1)}), bf16[1536,4096]{1,0:T(8,128)(2,1)}) %all-gather.8.cloned.1.call-update) | async-done | bytes 12582928 | tf_op jit(solution)/shard_map/all_gather | solution.py:129
  213.8 11.5 %fusion.3 = f32[1536,384]{1,0:T(8,128)} fusion(bf16[1536,4096]{1,0:T(8,128)(2,1)} %all-gather.8.cloned.1.call-done, bf16[1,4096,384]{2,1,0:T(8,128)(2,1)} %param.25), kind=kOutput, calls=%fused_computation.9 | convolution fusion | flops 4831838208 | bytes 18087936 | tf_op jit(solution)/shard_map/dot_general | solution.py:130
  225.3 20.0 %convolution_convert_fusion = bf16[1536,4096]{1,0:T(8,128)(2,1)} fusion(bf16[1,384,4096]{2,1,0:T(8,128)(2,1)S(1)} %copy-done, bf16[1536,4096]{1,0:T(8,128)(2,1)} %all-gather.8.cloned.1.call-done, bf16[1,4096,384]{2,1,0:T(8,128)(2,1)} %param.26, f32[1536,384]{1,0:T(8,128)} %fusion.3), kind=kOutput, calls=%fused_computation.3 | convolution fusion | flops 9673506816 | bytes 33816576 | tf_op jit(solution)/shard_map/dot_general | solution.py:134
  246.3 110.3 %reduce-scatter.3.cloned.1.call-done = bf16[48,4096]{1,0:T(8,128)(2,1)} async-done(((bf16[1536,4096]{1,0:T(8,128)(2,1)}), bf16[48,4096]{1,0:T(8,128)(2,1)}) %reduce-scatter.3.cloned.1.call-update) | async-done | bytes 393232 | tf_op jit(solution)/shard_map/reduce_scatter | solution.py:133
  356.5 3.0 convolution_convert_fusion.1
  359.6 39.0 %reduce-scatter.5.cloned.1.call-done = bf16[128,512]{1,0:T(8,128)(2,1)} async-done(((bf16[128,4096]{1,0:T(8,128)(2,1)}), bf16[128,512]{1,0:T(8,128)(2,1)}) %reduce-scatter.5.cloned.1.call-update) | async-done | bytes 131088 | tf_op jit(solution)/shard_map/reduce_scatter | solution.py:142
  (80 shorter events, 10.9 us)
Async XLA Ops:
  7.2 218.2 %copy-start = (bf16[1,384,4096]{2,1,0:T(8,128)(2,1)S(1)}, bf16[1,384,4096]{2,1,0:T(8,128)(2,1)}, u32[]{:S(2)}) copy-start(bf16[1,384,4096]{2,1,0:T(8,128)(2,1)} %param.27) | copy-start | bytes 9437188
  7.2 58.6 %all-gather.10.cloned.1.call-start = ((), (), s32[]{:S(2)}) async-start(), calls=%async_computation.6 | async-start | bytes 4325376 | tf_op jit(solution)/shard_map/all_gather | solution.py:12
  10.2 1.8 copy-start.1
  11.9 131.4 %all-gather.6.cloned.1.call-start = ((), (), s32[]{:S(2)}) async-start(), calls=%async_computation.2 | async-start | bytes 1179648 | tf_op jit(solution)/shard_map/all_gather | solution.py:116
  12.7 87.9 %copy-start.2 = (bf16[128,512]{0,1:T(8,128)(2,1)S(1)}, bf16[128,512]{0,1:T(8,128)(2,1)}, u32[]{:S(2)}) copy-start(bf16[128,512]{0,1:T(8,128)(2,1)} %copy-done.1) | copy-start | bytes 393220
  99.5 5.5 %copy-start.3 = (s32[128,2]{0,1:T(2,128)S(1)}, s32[128,2]{0,1:T(2,128)}, u32[]{:S(2)}) copy-start(s32[128,2]{0,1:T(2,128)} %param.28) | copy-start | bytes 3076
  105.0 108.8 %all-gather.8.cloned.1.call-start = ((), (), s32[]{:S(2)}) async-start(), calls=%async_computation.3 | async-start | bytes 12976128 | tf_op jit(solution)/shard_map/all_gather | solution.py:129
  147.4 209.1 %reduce-scatter.3.cloned.1.call-start = ((), (), s32[]{:S(2)}) async-start(), calls=%async_computation.4 | async-start | bytes 12976128 | tf_op jit(solution)/shard_map/reduce_scatter | solution.py:133
  245.3 0.7 copy-start.4
  245.4 153.2 %reduce-scatter.5.cloned.1.call-start = ((), (), s32[]{:S(2)}) async-start(), calls=%async_computation.5 | async-start | bytes 1179648 | tf_op jit(solution)/shard_map/reduce_scatter | solution.py:142
Sparse Core Ops, SparseCore 0:
  12.0 53.6 all-gather.9
  105.1 38.1 all-gather.5
  147.5 66.2 all-gather.7
  245.5 111.0 reduce-scatter.2
  359.7 38.8 reduce-scatter.4
where the time goes:
time: 406 us; the launch traced here: 405 us
  waiting for transfers between devices  278 us (68%)
  matrix products  43.4 us (11%)
  other arithmetic  40.5 us (10%)
  blocking collectives  21.7 us (5%)
  between operations  13.9 us (3%)
  local copies, waits for them, and re-layouts  5.99 us (1%)
    reduce_scatter x1, waiting for transfers between devices, on_device(): lax.psum_scatter(jnp.dot(hidden, down_here, preferred_element_type=jnp.fl...  110 us
    all_gather x1, waiting for transfers between devices, on_device(): token_piece = lax.all_gather(chosen, 'ctx', axis=0, tiled=True)  66.3 us
    reduce_scatter x1, waiting for transfers between devices, on_device(): lax.psum_scatter(spread.astype(jnp.bfloat16), 'exp', scatter_dimension=1,...  39 us
    all_gather x1, waiting for transfers between devices, on_device(): gathered = lax.all_gather(block_out, 'exp', axis=1, tiled=True)  37.9 us
    select_n x32, other arithmetic, lap(): return jax.tree.map(lambda a, b: jnp.where(reached, a, b), new, before)  32.4 us
    all_gather x1, waiting for transfers between devices, carried_in(): lax.all_gather(part.astype(kind), axis)  24.9 us
    all_gather x1, blocking collectives, carried_in(): lax.all_gather(part.astype(kind), axis)  21.7 us
    dot_general x1, matrix products, on_device(): jnp.dot(hidden, down_here, preferred_element_type=jnp.float32)  20 us
  transfers between devices with their start and end apart: 5, of which 5 were waited for; matrix products, arithmetic and copies ran while one was open for 2% of the time, Pallas kernels for 0%

commit v1 on v0

--- a/solution.py
+++ b/solution.py
@@ -4,6 +4,19 @@
 from jax.sharding import PartitionSpec as P
 
 precise = lax.Precision.HIGHEST
+
+
+def gather_around(x, axis, dim):
+    ways = lax.axis_size(axis)
+    up = [(d, (d + 1) % ways) for d in range(ways)]
+    down = [(d, (d - 1) % ways) for d in range(ways)]
+    earlier, later = ([x], [x])
+    for _ in range(ways // 2):
+        earlier.append(lax.ppermute(earlier[-1], axis, up))
+    for _ in range((ways - 1) // 2):
+        later.append(lax.ppermute(later[-1], axis, down))
+    line = jnp.concatenate([*earlier[::-1], *later[1:]], axis=dim)
+    return jnp.roll(line, (lax.axis_index(axis) - ways // 2) * x.shape[dim], axis=dim)
 
 
 def carried_in(shard, axis, combine, identity):
@@ -113,7 +126,7 @@
     )
     own_table = lax.dynamic_index_in_dim(tables, owner_index, 0, keepdims=False)
     own_weight = lax.dynamic_index_in_dim(weights_all, owner_index, 0, keepdims=False)
-    gathered = lax.all_gather(block_out, "exp", axis=1, tiled=True)
+    gathered = gather_around(block_out, "exp", 1)
     widened = gathered.astype(jnp.float32)
     ffn_input = (
         widened

time: 406 us -> 392 us (0.966)
  waiting for transfers between devices: 278 us -> 256 us
  starting transfers between devices: 0.21 us -> 12.1 us
    all_gather x1 -> x0, waiting for transfers between devices: 37.9 us -> none  [on_device(): gathered = lax.all_gather(block_out, 'exp', axis=1, tiled=True)]
    ppermute x0 -> x7, waiting for transfers between devices: none -> 13.8 us  [the longest x4 13.8 us: gather_around(): earlier.append(lax.ppermute(earlier[-1], axis, up))]
    ppermute x0 -> x7, starting transfers between devices: none -> 11.8 us  [the longest x3 10.1 us: gather_around(): later.append(lax.ppermute(later[-1], axis, down))]
  transfers between devices with their start and end apart: 5 -> 11, of which waited for: 5 -> 8; matrix products, arithmetic and copies ran while one was open for 2% -> 2% of each run, Pallas kernels for 0% -> 0%
where the time goes in v1:
time: 392 us; the launch traced here: 391 us
  waiting for transfers between devices  256 us (65%)
  matrix products  42.2 us (11%)
  other arithmetic  37.9 us (10%)
  blocking collectives  21.5 us (5%)
  between operations  14.1 us (4%)
  starting transfers between devices  12.1 us (3%)
  local copies, waits for them, and re-layouts  5.67 us (1%)
    reduce_scatter x1, waiting for transfers between devices, on_device(): lax.psum_scatter(jnp.dot(hidden, down_here, preferred_element_type=jnp.fl...  110 us
    all_gather x1, waiting for transfers between devices, on_device(): token_piece = lax.all_gather(chosen, 'ctx', axis=0, tiled=True)  67.7 us
    reduce_scatter x1, waiting for transfers between devices, on_device(): lax.psum_scatter(spread.astype(jnp.bfloat16), 'exp', scatter_dimension=1,...  38.9 us
    select_n x32, other arithmetic, lap(): return jax.tree.map(lambda a, b: jnp.where(reached, a, b), new, before)  32.4 us
    all_gather x1, waiting for transfers between devices, carried_in(): lax.all_gather(part.astype(kind), axis)  25.8 us
    all_gather x1, blocking collectives, carried_in(): lax.all_gather(part.astype(kind), axis)  21.5 us
    dot_general x1, matrix products, on_device(): jnp.dot(hidden, down_here, preferred_element_type=jnp.float32)  20 us
    ppermute x4, waiting for transfers between devices, gather_around(): earlier.append(lax.ppermute(earlier[-1], axis, up))  13.8 us
  transfers between devices with their start and end apart: 11, of which 8 were waited for; matrix products, arithmetic and copies ran while one was open for 2% of the time, Pallas kernels for 0%

profile of v1, /device:TPU:2, one launch (start us, length us, event | category | flops | bytes accessed | tf_op | source)
XLA Modules:
  0.0 390.9 jit_solution(16374780791976487889)
XLA Ops:
  8.5 1.0 copy.54
  9.6 1.7 convolution_convert_fusion.3
  12.0 21.5 %all-gather.1 = bf16[32,1,8]{2,1,0:T(2,128)(2,1)S(1)} all-gather(bf16[1,1,8]{2,1,0:T(2,128)(2,1)S(1)} %convert_bitcast_fusion), channel_id=1, replica_groups=mesh['ctx'=32,'exp'=8] {'ctx'}, dimensions={0}, use_global_device_ids=true | all-gather | bytes 528 | tf_op jit(solution)/shard_map/all_gather | solution.py:25
  33.6 1.7 convert_multiply_fusion.2
  35.3 1.8 copy.59
  37.7 1.5 fusion.54
  39.3 25.8 %all-gather.7.cloned.1.call-done = bf16[256,64,128]{2,1,0:T(8,128)(2,1)} async-done(((bf16[8,64,128]{2,1,0:T(8,128)(2,1)}), bf16[256,64,128]{2,1,0:T(8,128)(2,1)}) %all-gather.7.cloned.1.call-update) | async-done | bytes 4194320 | tf_op jit(solution)/shard_map/all_gather | solution.py:25
  65.1 33.8 %while.14 = (s32[]{:T(128)}, f32[8,64,128]{2,1,0:T(8,128)S(1)}, s32[]{:T(128)}, bf16[32,8]{1,0:T(8,128)(2,1)S(1)}, bf16[32,8,64,128]{3,2,1,0:T(8,128)(2,1)}, /*index=5*/s32[]{:T(128)}, s32[]{:T(128)}) while((s32[]{:T(128)}, f32[8,64,128]{2,1,0:T(8,128)S(1)}, s32[]{:T(128)}, bf16[32,8]{1,0:T(8,128)(2,1)S(1)}, ...), condition=%wide.region_2.3_spmd.clone, body=%wide.region_1.2_spmd.clone.sunk | while | flops 327692 | bytes 655545 | solution.py:42
  65.1 1.0 fusion.65
  66.2 1.0 fusion.65
  67.3 1.0 fusion.65
  68.3 1.0 fusion.65
  69.4 1.0 fusion.65
  70.4 1.0 fusion.65
  71.5 1.0 fusion.65
  72.5 1.0 fusion.65
  73.6 1.0 fusion.65
  75.7 1.0 fusion.65
  77.8 1.0 fusion.65
  78.9 1.0 fusion.65
  79.9 1.0 fusion.65
  81.0 1.0 fusion.65
  83.1 1.0 fusion.65
  85.2 1.0 fusion.65
  87.3 1.0 fusion.65
  89.4 1.0 fusion.65
  91.5 1.0 fusion.65
  93.7 1.0 fusion.65
  95.8 1.0 fusion.65
  97.9 1.0 fusion.65
  98.9 1.0 fusion.16
  100.0 1.8 multiply_reduce_fusion
  102.7 1.0 add_convert_fusion
  103.7 1.6 collective-permute-start
  105.3 5.6 %collective-permute-done = bf16[128,512]{1,0:T(8,128)(2,1)S(1)} collective-permute-done((bf16[128,512]{1,0:T(8,128)(2,1)S(1)}, bf16[128,512]{1,0:T(8,128)(2,1)S(1)}, u32[]{:S(2)}, u32[]{:S(2)}) %collective-permute-start) | collective-permute-done | bytes 131104 | tf_op jit(solution)/shard_map/ppermute | solution.py:15
  111.3 3.3 collective-permute-start.4
  114.5 2.7 collective-permute-done.1
  117.3 3.5 collective-permute-start.5
  120.7 2.7 collective-permute-done.2
  123.5 3.4 collective-permute-start.6
  126.9 2.7 collective-permute-done.3
  130.4 1.3 convolution_convert_fusion.2
  131.9 67.7 %all-gather.5.cloned.1.call-done = bf16[1536,4096]{1,0:T(8,128)(2,1)} async-done(((bf16[48,4096]{1,0:T(8,128)(2,1)}), bf16[1536,4096]{1,0:T(8,128)(2,1)}) %all-gather.5.cloned.1.call-update) | async-done | bytes 12582928 | tf_op jit(solution)/shard_map/all_gather | solution.py:142
  199.6 11.6 %fusion.3 = f32[1536,384]{1,0:T(8,128)} fusion(bf16[1536,4096]{1,0:T(8,128)(2,1)} %all-gather.5.cloned.1.call-done, bf16[1,4096,384]{2,1,0:T(8,128)(2,1)} %param.25), kind=kOutput, calls=%fused_computation.9 | convolution fusion | flops 4831838208 | bytes 18087936 | tf_op jit(solution)/shard_map/dot_general | solution.py:143
  211.1 20.0 %convolution_convert_fusion = bf16[1536,4096]{1,0:T(8,128)(2,1)} fusion(bf16[1,384,4096]{2,1,0:T(8,128)(2,1)S(1)} %copy-done, bf16[1536,4096]{1,0:T(8,128)(2,1)} %all-gather.5.cloned.1.call-done, bf16[1,4096,384]{2,1,0:T(8,128)(2,1)} %param.26, f32[1536,384]{1,0:T(8,128)} %fusion.3), kind=kOutput, calls=%fused_computation.3 | convolution fusion | flops 9673506816 | bytes 33816576 | tf_op jit(solution)/shard_map/dot_general | solution.py:147
  232.2 110.2 %reduce-scatter.3.cloned.1.call-done = bf16[48,4096]{1,0:T(8,128)(2,1)} async-done(((bf16[1536,4096]{1,0:T(8,128)(2,1)}), bf16[48,4096]{1,0:T(8,128)(2,1)}) %reduce-scatter.3.cloned.1.call-update) | async-done | bytes 393232 | tf_op jit(solution)/shard_map/reduce_scatter | solution.py:146
  342.4 3.0 convolution_convert_fusion.1
  345.4 38.9 %reduce-scatter.5.cloned.1.call-done = bf16[128,512]{1,0:T(8,128)(2,1)} async-done(((bf16[128,4096]{1,0:T(8,128)(2,1)}), bf16[128,512]{1,0:T(8,128)(2,1)}) %reduce-scatter.5.cloned.1.call-update) | async-done | bytes 131088 | tf_op jit(solution)/shard_map/reduce_scatter | solution.py:155
  (117 shorter events, 16.4 us)
Async XLA Ops:
  7.2 204.0 %copy-start = (bf16[1,384,4096]{2,1,0:T(8,128)(2,1)S(1)}, bf16[1,384,4096]{2,1,0:T(8,128)(2,1)}, u32[]{:S(2)}) copy-start(bf16[1,384,4096]{2,1,0:T(8,128)(2,1)} %param.27) | copy-start | bytes 9437188
  7.2 58.0 %all-gather.7.cloned.1.call-start = ((), (), s32[]{:S(2)}) async-start(), calls=%async_computation.5 | async-start | bytes 4325376 | tf_op jit(solution)/shard_map/all_gather | solution.py:25
  9.5 1.8 copy-start.2
  11.3 188.3 %all-gather.5.cloned.1.call-start = ((), (), s32[]{:S(2)}) async-start(), calls=%async_computation.2 | async-start | bytes 12976128 | tf_op jit(solution)/shard_map/all_gather | solution.py:142
  37.1 62.9 %copy-start.3 = (bf16[128,512]{0,1:T(8,128)(2,1)S(1)}, bf16[128,512]{0,1:T(8,128)(2,1)}, u32[]{:S(2)}) copy-start(bf16[128,512]{0,1:T(8,128)(2,1)} %copy-done.2) | copy-start | bytes 393220
  98.9 3.8 copy-start.7
  98.9 6.4 %copy-start.6 = (s32[128,2]{0,1:T(2,128)S(1)}, s32[128,2]{0,1:T(2,128)}, u32[]{:S(2)}) copy-start(s32[128,2]{0,1:T(2,128)} %param.28) | copy-start | bytes 3076
  103.7 26.2 %copy-start.1 = (bf16[128,512]{1,0:T(8,128)(2,1)}, bf16[128,512]{1,0:T(8,128)(2,1)S(1)}, u32[]{:S(2)}) copy-start(bf16[128,512]{1,0:T(8,128)(2,1)S(1)} %add_convert_fusion) | copy-start | bytes 393220
  103.7 7.3 %collective-permute-start = (bf16[128,512]{1,0:T(8,128)(2,1)S(1)}, bf16[128,512]{1,0:T(8,128)(2,1)S(1)}, u32[]{:S(2)}, u32[]{:S(2)}) collective-permute-start(bf16[128,512]{1,0:T(8,128)(2,1)S(1)} %add_convert_fusion), channel_id=1, source_target_pairs={{0,1},{1,2},{2,3},{3,4},{4,5},{5,6},{6,7},{7,0},{8,9},{9,10},{10,1... | collective-permute-start | bytes 393224 | tf_op jit(solution)/shard_map/ppermute | solution.py:15
  111.0 6.3 %collective-permute-start.1 = (bf16[128,512]{1,0:T(8,128)(2,1)S(1)}, bf16[128,512]{1,0:T(8,128)(2,1)S(1)}, u32[]{:S(2)}, u32[]{:S(2)}) collective-permute-start(bf16[128,512]{1,0:T(8,128)(2,1)S(1)} %collective-permute-done), channel_id=1, source_target_pairs={{0,1},{1,2},{2,3},{3,4},{4,5},{5,6},{6,7},{7,0},{8,9},{9,10},{10,1... | collective-permute-start | bytes 393224 | tf_op jit(solution)/shard_map/ppermute | solution.py:15
  111.3 6.0 %collective-permute-start.4 = (bf16[128,512]{1,0:T(8,128)(2,1)S(1)}, bf16[128,512]{1,0:T(8,128)(2,1)S(1)}, u32[]{:S(2)}, u32[]{:S(2)}) collective-permute-start(bf16[128,512]{1,0:T(8,128)(2,1)S(1)} %add_convert_fusion), channel_id=1, source_target_pairs={{0,7},{1,0},{2,1},{3,2},{4,3},{5,4},{6,5},{7,6},{8,15},{9,8},{10,9... | collective-permute-start | bytes 393224 | tf_op jit(solution)/shard_map/ppermute | solution.py:17
  117.3 6.2 %collective-permute-start.2 = (bf16[128,512]{1,0:T(8,128)(2,1)S(1)}, bf16[128,512]{1,0:T(8,128)(2,1)S(1)}, u32[]{:S(2)}, u32[]{:S(2)}) collective-permute-start(bf16[128,512]{1,0:T(8,128)(2,1)S(1)} %collective-permute-done.1), channel_id=1, source_target_pairs={{0,1},{1,2},{2,3},{3,4},{4,5},{5,6},{6,7},{7,0},{8,9},{9,10},{10,1... | collective-permute-start | bytes 393224 | tf_op jit(solution)/shard_map/ppermute | solution.py:15
  117.3 6.2 %collective-permute-start.5 = (bf16[128,512]{1,0:T(8,128)(2,1)S(1)}, bf16[128,512]{1,0:T(8,128)(2,1)S(1)}, u32[]{:S(2)}, u32[]{:S(2)}) collective-permute-start(bf16[128,512]{1,0:T(8,128)(2,1)S(1)} %collective-permute-done.4), channel_id=1, source_target_pairs={{0,7},{1,0},{2,1},{3,2},{4,3},{5,4},{6,5},{7,6},{8,15},{9,8},{10,9... | collective-permute-start | bytes 393224 | tf_op jit(solution)/shard_map/ppermute | solution.py:17
  123.4 6.2 %collective-permute-start.3 = (bf16[128,512]{1,0:T(8,128)(2,1)S(1)}, bf16[128,512]{1,0:T(8,128)(2,1)S(1)}, u32[]{:S(2)}, u32[]{:S(2)}) collective-permute-start(bf16[128,512]{1,0:T(8,128)(2,1)S(1)} %collective-permute-done.2), channel_id=1, source_target_pairs={{0,1},{1,2},{2,3},{3,4},{4,5},{5,6},{6,7},{7,0},{8,9},{9,10},{10,1... | collective-permute-start | bytes 393224 | tf_op jit(solution)/shard_map/ppermute | solution.py:15
  123.5 6.8 %copy-start.4 = (pred[8,48,128]{2,1,0:T(8,128)(4,1)}, pred[8,48,128]{2,1,0:T(8,128)(4,1)S(1)}, u32[]{:S(2)}) copy-start(pred[8,48,128]{2,1,0:T(8,128)(4,1)S(1)} %fusion.39) | copy-start | bytes 147460
  123.5 6.3 %collective-permute-start.6 = (bf16[128,512]{1,0:T(8,128)(2,1)S(1)}, bf16[128,512]{1,0:T(8,128)(2,1)S(1)}, u32[]{:S(2)}, u32[]{:S(2)}) collective-permute-start(bf16[128,512]{1,0:T(8,128)(2,1)S(1)} %collective-permute-done.5), channel_id=1, source_target_pairs={{0,7},{1,0},{2,1},{3,2},{4,3},{5,4},{6,5},{7,6},{8,15},{9,8},{10,9... | collective-permute-start | bytes 393224 | tf_op jit(solution)/shard_map/ppermute | solution.py:17
  129.7 0.7 copy-start.9
  131.7 210.7 %reduce-scatter.3.cloned.1.call-start = ((), (), s32[]{:S(2)}) async-start(), calls=%async_computation.3 | async-start | bytes 12976128 | tf_op jit(solution)/shard_map/reduce_scatter | solution.py:146
  231.2 0.7 copy-start.8
  231.2 0.8 copy-start.5
  231.2 153.2 %reduce-scatter.5.cloned.1.call-start = ((), (), s32[]{:S(2)}) async-start(), calls=%async_computation.4 | async-start | bytes 1179648 | tf_op jit(solution)/shard_map/reduce_scatter | solution.py:155
Sparse Core Ops, SparseCore 0:
  11.4 53.6 all-gather.6
  131.8 67.7 all-gather.4
  231.3 111.0 reduce-scatter.2
  345.6 38.7 reduce-scatter.4
